TPU v7x, 32 devices: a whole 2x2x4 slice. The times are simulated.
32 devices in a mesh: patch: 8 (over z, y), band: 4 (over x, core).
Axes of the slice: x: 2, y: 2, z: 4, core: 2. Of those that a mesh axis runs over, the one named last changes fastest.
Arguments:
- exposures: float32 [64, 256, 128], P(('band', 'patch')), parts along dimension 0, may hold values from -6 to 6
- variance: float32 [64, 256, 128], P(('band', 'patch')), parts along dimension 0, may hold values from 0.01 to 60, as said below
- mask_bits: int32 [64, 256, 128], P(('band', 'patch')), parts along dimension 0, may hold values from 0 to 4095
- kernel_coeffs: float32 [64, 27, 6], P(('band', 'patch')), parts along dimension 0, may hold values from -3 to 3
- ccd_visit: int32 [64, 1], P(('band', 'patch')), parts along dimension 0, may hold values from 0 to 7
- strip_patch: int32 [2048, 1], P(('band', 'patch')), parts along dimension 0, may hold values from 0 to 7, as said below
- strip_row: int32 [2048], P(('band', 'patch')), parts along dimension 0, may hold values from 0 to 120
- strip_col: int32 [2048], P(('band', 'patch')), parts along dimension 0, may hold values from 0 to 384
Outputs:
- coadd_image: float32 [32, 128, 512], P(('band', 'patch')), parts along dimension 0
- weight_map: float32 [32, 128, 512], P(('band', 'patch')), parts along dimension 0
There are 4 independent parts, one for each index of `band`. A program takes and returns all parts, laid end to end along the dimension named above; each array names one. Nothing has to cross between parts.
Inputs may be any that keep to these rules, and one draw needn't show every extreme that they name: `variance`: Positive. `ccd_visit`: every visit has at least one CCD. `strip_patch`: among the strips of one device (aligned blocks of 64 rows) no patch is named more than 16 times; one patch is named exactly 16 times in every block.
All inputs are finite; a program needn't handle non-finite values.
Results may differ from a plain program's by a relative error of at most 0.00011.
Values sent between devices are 32-bit elements; how exact they have to be, the bound alone decides.
No kernel may reach another device: no remote copies, remote signals or barrier semaphores. Data moves between devices by JAX's collectives and lax.ppermute only.
A program may use at most 64 MiB of HBM per device.

v0:
```python
import math
import jax
import jax.numpy as jnp
from jax import lax
from jax.sharding import PartitionSpec as P

PH = 128
PW = 512
KS = 21
VISITS = 8
gauss_widths = (0.75, 1.5, 3.0)
largest_value = lax.Precision.HIGHEST
mxu_value = lax.Precision.HIGH


def tap_values(offsets, kernel_half_width):
    support = jnp.arange(-kernel_half_width, kernel_half_width + 1).astype(jnp.float32)
    inside = (jnp.abs(offsets) <= kernel_half_width).astype(jnp.float32)
    tables = []
    for spread in gauss_widths:
        gauss_total = jnp.sum(jnp.exp(-support * support / (2.0 * spread * spread)))
        profile = jnp.exp(-offsets * offsets / (2.0 * spread * spread)) / gauss_total * inside
        scaled = offsets / spread
        tables.append(jnp.stack([profile, profile * scaled, profile * scaled * scaled]))
    return jnp.stack(tables)


def row_filters(row_count, kernel_half_width):
    row_ids = jnp.arange(row_count)[:, None]
    window_ids = jnp.arange(row_count + 2 * kernel_half_width)[None, :]
    return tap_values(
        (window_ids - row_ids - kernel_half_width).astype(jnp.float32), kernel_half_width
    )


def column_filters(column_count, kernel_half_width):
    source = jnp.arange(column_count)[:, None]
    target_patch = jnp.arange(column_count)[None, :]
    return tap_values((source - target_patch).astype(jnp.float32), kernel_half_width)


def convolve_all(padded, kernel_coeffs, height):
    kernel_half_width = KS // 2
    n, _, columns = padded.shape
    rows = row_filters(height, kernel_half_width).reshape(9, height, height + 2 * kernel_half_width)
    smooth = jnp.einsum("krj,njx->nkrx", rows, padded, precision=mxu_value)
    col_ops = column_filters(columns, kernel_half_width)
    x_line = 2.0 * jnp.arange(columns).astype(jnp.float32) / (columns - 1) - 1.0
    coef = kernel_coeffs.reshape(n, 3, 3, 3, 6)
    c = [coef[..., p, None] for p in range(6)]
    fx = jnp.stack(
        [
            c[0] + c[1] * x_line + c[3] * (x_line * x_line),
            c[2] + c[4] * x_line,
            jnp.broadcast_to(c[5], c[0].shape[:-1] + (columns,)),
        ],
        axis=4,
    )
    mixed = jnp.sum(col_ops[None, :, None, :, :, None, :] * fx[:, :, :, :, None, :, :], axis=3)
    mixed = mixed.reshape(n, 9, columns, 3 * columns)
    fields = jnp.einsum("nkry,nkyz->nrz", smooth, mixed, precision=mxu_value)
    y_line = (2.0 * jnp.arange(height).astype(jnp.float32) / (height - 1) - 1.0)[None, :, None]
    return (
        fields[:, :, :columns]
        + y_line * fields[:, :, columns : 2 * columns]
        + y_line * y_line * fields[:, :, 2 * columns :]
    )


def place_slots(flux_flat, weight_flat, offsets, patch_rows, patch_cols):
    slot_total, strip_rows, columns = flux_flat.shape
    group = math.gcd(slot_total, 16)
    pairs = jnp.stack([flux_flat, weight_flat], axis=1).reshape(
        slot_total // group, group, 2, strip_rows, columns
    )
    grouped_offsets = offsets.reshape(slot_total // group, group, offsets.shape[1])
    target_cols = jnp.arange(patch_cols)
    source_cols = jnp.arange(columns)
    target_rows = jnp.arange(patch_rows)
    source_rows = jnp.arange(strip_rows)

    def place_group(total, item):
        pixel_block_tile, block_offsets = item
        column_selection = (
            target_cols[None, None, :]
            == block_offsets[:, 1][:, None, None] + source_cols[None, :, None]
        ).astype(jnp.float32)
        row_select = (
            target_rows[None, :, None]
            == block_offsets[:, 0][:, None, None] + source_rows[None, None, :]
        ).astype(jnp.float32)
        broadened_width = jnp.einsum(
            "vmwn,vny->vmwy", pixel_block_tile, column_selection, precision=largest_value
        )
        return (
            total
            + jnp.einsum("gri,gkip->krp", row_select, broadened_width, precision=largest_value),
            None,
        )

    start = jnp.zeros((2, patch_rows, patch_cols), jnp.float32)
    placed, _ = lax.scan(place_group, start, (pairs, grouped_offsets))
    return (placed[0], placed[1])


def shards(
    exposures, variance, mask_bits, kernel_coeffs, ccd_visit, strip_patch, strip_row, strip_col
):
    ccd_count, height, columns = exposures.shape
    strip_total = strip_patch.shape[0]
    per_ccd = strip_total // ccd_count
    strip_rows = height // per_ccd
    devices = lax.axis_size("patch")
    capacity = 2 * strip_total // devices
    kernel_half_width = KS // 2
    usable = (jnp.bitwise_and(mask_bits, 3) != 3).astype(jnp.float32)
    visit_hot = (ccd_visit == jnp.arange(VISITS)[None, :]).astype(jnp.float32)
    local_count = jnp.sum(jnp.sum(usable, axis=(1, 2))[:, None] * visit_hot, axis=0)
    local_load = jnp.sum(jnp.sum(usable * variance, axis=(1, 2))[:, None] * visit_hot, axis=0)
    destination = strip_patch[:, 0]
    strip_ids = jnp.arange(strip_total)
    earlier = strip_ids[None, :] < strip_ids[:, None]
    same_target = destination[None, :] == destination[:, None]
    slot_rank = jnp.sum(jnp.logical_and(earlier, same_target).astype(jnp.int32), axis=1)
    slot_index = destination * capacity + slot_rank
    slot_total = devices * capacity
    chooser = (slot_index[None, :] == jnp.arange(slot_total)[:, None]).astype(jnp.float32)
    padded = jnp.pad(exposures, ((0, 0), (kernel_half_width, kernel_half_width), (0, 0)))
    convolved = convolve_all(padded, kernel_coeffs, height)
    tiles = jnp.concatenate(
        [
            (usable * convolved).reshape(strip_total, strip_rows, columns),
            usable.reshape(strip_total, strip_rows, columns),
        ],
        axis=1,
    ).reshape(strip_total, 2 * strip_rows * columns)
    packed = jnp.dot(chooser, tiles, precision=largest_value).reshape(
        devices, capacity * 2 * strip_rows, columns
    )
    strip_visit = jnp.repeat(ccd_visit[:, 0], per_ccd)
    placement = jnp.stack([strip_row, strip_col, strip_visit], axis=1).astype(jnp.float32)
    slot_meta = jnp.dot(chooser, placement, precision=largest_value).reshape(devices, capacity, 3)
    meta = jnp.zeros((devices, 8, columns), jnp.float32)
    meta = meta.at[:, 0:3, :capacity].set(jnp.swapaxes(slot_meta, 1, 2))
    meta = meta.at[:, 3, :VISITS].set(jnp.broadcast_to(local_count, (devices, VISITS)))
    meta = meta.at[:, 4, :VISITS].set(jnp.broadcast_to(local_load, (devices, VISITS)))
    payload = jnp.concatenate([packed, meta], axis=1)
    got = lax.all_to_all(payload, "patch", split_axis=0, concat_axis=0, tiled=True)
    body_rows = capacity * 2 * strip_rows
    got_meta = got[:, body_rows:, :]
    visit_count = jnp.sum(got_meta[:, 3, :VISITS], axis=0)
    visit_load = jnp.sum(got_meta[:, 4, :VISITS], axis=0)
    visit_weight = (visit_count + 1.0) / (visit_load + 1.0)
    slot_rows = got_meta[:, 0, :capacity].reshape(slot_total).astype(jnp.int32)
    slot_cols = got_meta[:, 1, :capacity].reshape(slot_total).astype(jnp.int32)
    slot_visit = got_meta[:, 2, :capacity].reshape(slot_total).astype(jnp.int32)
    slot_hot = (slot_visit[:, None] == jnp.arange(VISITS)[None, :]).astype(jnp.float32)
    slot_weight = jnp.sum(slot_hot * visit_weight[None, :], axis=1)
    body = got[:, :body_rows, :].reshape(slot_total, 2, strip_rows, columns)
    body = body * slot_weight[:, None, None, None]
    offsets = jnp.stack([slot_rows, slot_cols], axis=1)
    numerator, weight_map = place_slots(body[:, 0], body[:, 1], offsets, PH, PW)
    coadd_image = numerator / jnp.maximum(weight_map, 1.0)
    return (coadd_image[None], weight_map[None])


def solution(mesh):
    return jax.shard_map(
        shards,
        mesh=mesh,
        in_specs=(
            P(("band", "patch"), None, None),
            P(("band", "patch"), None, None),
            P(("band", "patch"), None, None),
            P(("band", "patch"), None, None),
            P(("band", "patch"), None),
            P(("band", "patch"), None),
            P(("band", "patch")),
            P(("band", "patch")),
        ),
        out_specs=(P(("band", "patch"), None, None), P(("band", "patch"), None, None)),
        check_vma=False,
    )
```

profile of v0, /device:TPU:0, one launch (start us, length us, event | category | flops | bytes accessed | tf_op | source)
XLA Modules:
  0.0 92.9 jit_solution(15024950080672934833)
XLA Ops:
  6.8 1.6 %divide_select_fusion.2 = (f32[1,256,276]{1,2,0:T(8,128)}, f32[1,256,276]{1,2,0:T(8,128)}) fusion(f32[]{:T(128)} %exponential_reduce_fusion.2), kind=kLoop, calls=%fused_computation.40 | loop fusion | flops 918528 | bytes 565252 | tf_op jit(solution)/shard_map/mul | solution.py:22
  8.5 1.5 %fusion.30 = f32[1,256,276]{1,2,0:T(8,128)} fusion(f32[]{:T(128)} %exponential_reduce_fusion.2), kind=kLoop, calls=%fused_computation.49 | loop fusion | flops 847872 | bytes 282628 | tf_op jit(solution)/shard_map/mul | solution.py:24
  10.0 1.6 %divide_select_fusion.1 = (f32[1,256,276]{1,2,0:T(8,128)}, f32[1,256,276]{1,2,0:T(8,128)}) fusion(f32[]{:T(128)} %exponential_reduce_fusion.1), kind=kLoop, calls=%fused_computation.39 | loop fusion | flops 918528 | bytes 565252 | tf_op jit(solution)/shard_map/mul | solution.py:22
  11.6 1.5 %fusion.32 = f32[1,256,276]{1,2,0:T(8,128)} fusion(f32[]{:T(128)} %exponential_reduce_fusion.1), kind=kLoop, calls=%fused_computation.51 | loop fusion | flops 847872 | bytes 282628 | tf_op jit(solution)/shard_map/mul | solution.py:24
  13.1 1.6 %divide_select_fusion = (f32[1,256,276]{1,2,0:T(8,128)}, f32[1,256,276]{1,2,0:T(8,128)}) fusion(f32[]{:T(128)} %exponential_reduce_fusion), kind=kLoop, calls=%fused_computation.38 | loop fusion | flops 918528 | bytes 565252 | tf_op jit(solution)/shard_map/mul | solution.py:22
  14.7 1.5 %fusion.28 = f32[1,256,276]{1,2,0:T(8,128)} fusion(f32[]{:T(128)} %exponential_reduce_fusion), kind=kLoop, calls=%fused_computation.47 | loop fusion | flops 847872 | bytes 282628 | tf_op jit(solution)/shard_map/mul | solution.py:24
  18.6 2.7 %multiply_reduce_fusion = f32[2,3,3,128,3,128]{5,3,4,2,1,0:T(8,128)} fusion(f32[2,3,3,3,3,128]{5,4,3,2,1,0:T(4,128)S(1)} %pad_maximum_fusion.4, f32[3,3,128,128]{3,2,1,0:T(8,128)S(1)} %pad_maximum_fusion.2), kind=kLoop, calls=%fused_computation.20 | loop fusion | flops 4423680 | bytes 4211712 | tf_op jit(solution)/shard_map/reduce_sum | solution.py:59
  21.3 3.3 %copy.81 = f32[2,3,3,128,3,128]{3,5,4,2,1,0:T(8,128)S(1)} copy(f32[2,3,3,128,3,128]{5,3,4,2,1,0:T(8,128)} %multiply_reduce_fusion) | data formatting | bytes 7077888 | tf_op jit(solution)/shard_map/reduce_sum | solution.py:59
  24.7 1.3 %maximum_bitcast_fusion = f32[1,3,256,276]{2,3,1,0:T(8,128)S(1)} fusion(f32[1,256,276]{1,2,0:T(8,128)} %get-tuple-element.195, f32[1,256,276]{1,2,0:T(8,128)} %fusion.30, f32[1,256,276]{1,2,0:T(8,128)} %get-tuple-element.194), kind=kLoop, calls=%fused_computation.26 | loop fusion | flops 423936 | bytes 1695744 | tf_op jit(solution)/shard_map/stack | solution.py:25
  26.0 1.2 %maximum_bitcast_fusion.1 = f32[1,3,256,276]{2,3,1,0:T(8,128)S(1)} fusion(f32[1,256,276]{1,2,0:T(8,128)} %get-tuple-element.191, f32[1,256,276]{1,2,0:T(8,128)} %fusion.32, f32[1,256,276]{1,2,0:T(8,128)} %get-tuple-element.190), kind=kLoop, calls=%fused_computation.27 | loop fusion | flops 423936 | bytes 1695744 | tf_op jit(solution)/shard_map/stack | solution.py:25
  28.2 2.2 %fusion.25 = f32[2,128,9,256]{3,1,2,0:T(8,128)S(1)} fusion(f32[9,256,276,1]{1,2,0,3:T(8,128)S(1)} %bitcast.103, f32[2,256,128]{2,1,0:T(8,128)S(1)} %copy-done.3), kind=kOutput, calls=%fused_computation.36 | convolution fusion | flops 976748544 | bytes 5165056 | tf_op jit(solution)/shard_map/krj,njx->nkrx/dot_general | solution.py:46
  30.5 4.1 %fusion.19 = f32[2,256,384]{2,1,0:T(8,128)S(1)} fusion(f32[2,9,128,384]{2,3,1,0:T(8,128)S(1)} %bitcast.102, f32[2,128,9,256]{3,1,2,0:T(8,128)S(1)} %fusion.25), kind=kOutput, calls=%fused_computation.24 | convolution fusion | flops 1358954496 | bytes 6684672 | tf_op jit(solution)/shard_map/nkry,nkyz->nrz/dot_general | solution.py:61
  37.4 1.1 %pad_maximum_fusion.1 = f32[8,264,128]{2,1,0:T(8,128)} fusion(f32[8,8,128]{2,1,0:T(8,128)S(1)} %scatter.14, f32[8,256,128]{2,1,0:T(8,128)S(1)} %reshape.602), kind=kLoop, calls=%fused_computation.25 | loop fusion | flops 270336 | bytes 2162688 | tf_op jit(solution)/shard_map/concatenate | solution.py:147
  38.5 7.3 %all-to-all-start = ((f32[8,264,128]{2,1,0:T(8,128)}), f32[8,264,128]{2,1,0:T(8,128)S(1)}, u32[]{:S(2)}, u32[]{:S(2)}) async-start(f32[8,264,128]{2,1,0:T(8,128)} %pad_maximum_fusion.1), calls=%async_computation | async-start | bytes 2162688 | tf_op jit(solution)/shard_map/all_to_all | solution.py:148
  45.8 26.5 %all-to-all-done = f32[8,264,128]{2,1,0:T(8,128)S(1)} async-done(((f32[8,264,128]{2,1,0:T(8,128)}), f32[8,264,128]{2,1,0:T(8,128)S(1)}, u32[]{:S(2)}, u32[]{:S(2)}) %all-to-all-start) | async-done | bytes 1081376 | tf_op jit(solution)/shard_map/all_to_all | solution.py:148
  72.9 19.0 %while.16 = (s32[]{:T(128)}, f32[2,128,512]{1,2,0:T(8,128)S(1)}, f32[8,16,2,8,128]{4,3,2,1,0:T(8,128)S(1)}, s32[8,16,2]{1,0,2:T(8,128)S(1)}, s32[]{:T(128)}, /*index=5*/s32[]{:T(128)}) while((s32[]{:T(128)}, f32[2,128,512]{1,2,0:T(8,128)S(1)}, f32[8,16,2,8,128]{4,3,2,1,0:T(8,128)S(1)}, s32[8,16,2]{1,0,2:T(8,128)S(1)}, ...), condition=%wide.region_13.14_spmd.clone.clone, body=%wide.region_12.13_spmd.clone.clone.sunk | while | flops 403982464 | bytes 2246359 | solution.py:102
  73.0 1.5 %fusion.71 = f32[16,2,8,512]{3,2,1,0:T(8,128)S(1)} fusion(s32[16,128]{1,0:T(8,128)S(1)} %iota_add_fusion.4, f32[8,16,2,8,128]{4,3,2,1,0:T(8,128)S(1)} %get-tuple-element.243, s32[]{:T(128)} %get-tuple-element.235), kind=kOutput, calls=%fused_computation.5.clone.1 | convolution fusion | flops 202375168 | bytes 663556 | tf_op jit(solution)/shard_map/while/body/eval_jaxpr/vmwn,vny->vmwy/dot_general | solution.py:92
  75.4 1.5 %fusion.71 = f32[16,2,8,512]{3,2,1,0:T(8,128)S(1)} fusion(s32[16,128]{1,0:T(8,128)S(1)} %iota_add_fusion.4, f32[8,16,2,8,128]{4,3,2,1,0:T(8,128)S(1)} %get-tuple-element.243, s32[]{:T(128)} %get-tuple-element.235), kind=kOutput, calls=%fused_computation.5.clone.1 | convolution fusion | flops 202375168 | bytes 663556 | tf_op jit(solution)/shard_map/while/body/eval_jaxpr/vmwn,vny->vmwy/dot_general | solution.py:92
  77.8 1.5 %fusion.71 = f32[16,2,8,512]{3,2,1,0:T(8,128)S(1)} fusion(s32[16,128]{1,0:T(8,128)S(1)} %iota_add_fusion.4, f32[8,16,2,8,128]{4,3,2,1,0:T(8,128)S(1)} %get-tuple-element.243, s32[]{:T(128)} %get-tuple-element.235), kind=kOutput, calls=%fused_computation.5.clone.1 | convolution fusion | flops 202375168 | bytes 663556 | tf_op jit(solution)/shard_map/while/body/eval_jaxpr/vmwn,vny->vmwy/dot_general | solution.py:92
  80.1 1.5 %fusion.71 = f32[16,2,8,512]{3,2,1,0:T(8,128)S(1)} fusion(s32[16,128]{1,0:T(8,128)S(1)} %iota_add_fusion.4, f32[8,16,2,8,128]{4,3,2,1,0:T(8,128)S(1)} %get-tuple-element.243, s32[]{:T(128)} %get-tuple-element.235), kind=kOutput, calls=%fused_computation.5.clone.1 | convolution fusion | flops 202375168 | bytes 663556 | tf_op jit(solution)/shard_map/while/body/eval_jaxpr/vmwn,vny->vmwy/dot_general | solution.py:92
  82.5 1.5 %fusion.71 = f32[16,2,8,512]{3,2,1,0:T(8,128)S(1)} fusion(s32[16,128]{1,0:T(8,128)S(1)} %iota_add_fusion.4, f32[8,16,2,8,128]{4,3,2,1,0:T(8,128)S(1)} %get-tuple-element.243, s32[]{:T(128)} %get-tuple-element.235), kind=kOutput, calls=%fused_computation.5.clone.1 | convolution fusion | flops 202375168 | bytes 663556 | tf_op jit(solution)/shard_map/while/body/eval_jaxpr/vmwn,vny->vmwy/dot_general | solution.py:92
  84.9 1.5 %fusion.71 = f32[16,2,8,512]{3,2,1,0:T(8,128)S(1)} fusion(s32[16,128]{1,0:T(8,128)S(1)} %iota_add_fusion.4, f32[8,16,2,8,128]{4,3,2,1,0:T(8,128)S(1)} %get-tuple-element.243, s32[]{:T(128)} %get-tuple-element.235), kind=kOutput, calls=%fused_computation.5.clone.1 | convolution fusion | flops 202375168 | bytes 663556 | tf_op jit(solution)/shard_map/while/body/eval_jaxpr/vmwn,vny->vmwy/dot_general | solution.py:92
  87.3 1.5 %fusion.71 = f32[16,2,8,512]{3,2,1,0:T(8,128)S(1)} fusion(s32[16,128]{1,0:T(8,128)S(1)} %iota_add_fusion.4, f32[8,16,2,8,128]{4,3,2,1,0:T(8,128)S(1)} %get-tuple-element.243, s32[]{:T(128)} %get-tuple-element.235), kind=kOutput, calls=%fused_computation.5.clone.1 | convolution fusion | flops 202375168 | bytes 663556 | tf_op jit(solution)/shard_map/while/body/eval_jaxpr/vmwn,vny->vmwy/dot_general | solution.py:92
  89.6 1.5 %fusion.71 = f32[16,2,8,512]{3,2,1,0:T(8,128)S(1)} fusion(s32[16,128]{1,0:T(8,128)S(1)} %iota_add_fusion.4, f32[8,16,2,8,128]{4,3,2,1,0:T(8,128)S(1)} %get-tuple-element.243, s32[]{:T(128)} %get-tuple-element.235), kind=kOutput, calls=%fused_computation.5.clone.1 | convolution fusion | flops 202375168 | bytes 663556 | tf_op jit(solution)/shard_map/while/body/eval_jaxpr/vmwn,vny->vmwy/dot_general | solution.py:92
  (130 shorter events, 20.7 us)
Async XLA Ops:
  0.6 15.6 %copy-start.6 = (f32[2,27,6]{1,0,2:T(2,128)S(1)}, f32[2,27,6]{1,0,2:T(2,128)}, u32[]{:S(2)}) copy-start(f32[2,27,6]{1,0,2:T(2,128)} %param.19) | copy-start | bytes 3892
  24.6 2.5 %copy-start = (f32[1,256,276]{1,2,0:T(8,128)S(1)}, f32[1,256,276]{1,2,0:T(8,128)}, u32[]{:S(2)}) copy-start(f32[1,256,276]{1,2,0:T(8,128)} %fusion.28) | copy-start | bytes 847876
  24.7 2.5 %copy-start.1 = (f32[1,256,276]{1,2,0:T(8,128)S(1)}, f32[1,256,276]{1,2,0:T(8,128)}, u32[]{:S(2)}) copy-start(f32[1,256,276]{1,2,0:T(8,128)} %get-tuple-element.186) | copy-start | bytes 847876
  24.7 2.5 %copy-start.2 = (f32[1,256,276]{1,2,0:T(8,128)S(1)}, f32[1,256,276]{1,2,0:T(8,128)}, u32[]{:S(2)}) copy-start(f32[1,256,276]{1,2,0:T(8,128)} %get-tuple-element.187) | copy-start | bytes 847876
  27.3 1.0 %copy-start.3 = (f32[2,256,128]{2,1,0:T(8,128)S(1)}, f32[2,256,128]{2,1,0:T(8,128)}, u32[]{:S(2)}) copy-start(f32[2,256,128]{2,1,0:T(8,128)} %param.16) | copy-start | bytes 786436
  30.5 4.1 %copy-start.5 = (s32[2,256,128]{2,1,0:T(8,128)S(1)}, s32[2,256,128]{2,1,0:T(8,128)}, u32[]{:S(2)}) copy-start(s32[2,256,128]{2,1,0:T(8,128)} %param.18) | copy-start | bytes 786436
  30.5 4.3 %copy-start.8 = (s32[64,1]{0,1:T(1,128)S(1)}, s32[64,1]{0,1:T(1,128)}, u32[]{:S(2)}) copy-start(s32[64,1]{0,1:T(1,128)} %param.21) | copy-start | bytes 772
  34.7 1.2 %copy-start.4 = (f32[2,256,128]{2,1,0:T(8,128)S(1)}, f32[2,256,128]{2,1,0:T(8,128)}, u32[]{:S(2)}) copy-start(f32[2,256,128]{2,1,0:T(8,128)} %param.17) | copy-start | bytes 786436
  34.8 1.4 %copy-start.7 = (s32[2,1]{0,1:T(1,128)S(1)}, s32[2,1]{0,1:T(1,128)}, u32[]{:S(2)}) copy-start(s32[2,1]{0,1:T(1,128)} %param.20) | copy-start | bytes 28
  34.8 1.5 %copy-start.9 = (s32[64]{0:T(128)S(1)}, s32[64]{0:T(128)}, u32[]{:S(2)}) copy-start(s32[64]{0:T(128)} %param.23) | copy-start | bytes 772
  34.8 1.5 %copy-start.10 = (s32[64]{0:T(128)S(1)}, s32[64]{0:T(128)}, u32[]{:S(2)}) copy-start(s32[64]{0:T(128)} %param.22) | copy-start | bytes 772
  38.5 33.8 %all-to-all-start = ((f32[8,264,128]{2,1,0:T(8,128)}), f32[8,264,128]{2,1,0:T(8,128)S(1)}, u32[]{:S(2)}, u32[]{:S(2)}) async-start(f32[8,264,128]{2,1,0:T(8,128)} %pad_maximum_fusion.1), calls=%async_computation | async-start | bytes 2162688 | tf_op jit(solution)/shard_map/all_to_all | solution.py:148
where the time goes:
time: 93.3 us; the launch traced here: 92.9 us
  waiting for transfers between devices  26.5 us (28%)
  other arithmetic  25.6 us (27%)
  matrix products  24.6 us (26%)
  local copies, waits for them, and re-layouts  7.52 us (8%)
  starting transfers between devices  7.31 us (8%)
  between operations  1.13 us (1%)
    all_to_all x1, waiting for transfers between devices, shards(): lax.all_to_all(payload, 'patch', split_axis=0, concat_axis=0, tiled=True)  26.5 us
    dot_general x8, matrix products, place_group(): jnp.einsum('vmwn,vny->vmwy', pixel_block_tile, column_selection, precisio...  11.7 us
    all_to_all x1, starting transfers between devices, shards(): lax.all_to_all(payload, 'patch', split_axis=0, concat_axis=0, tiled=True)  7.31 us
    mul x6, other arithmetic, tap_values(): jnp.exp(-offsets * offsets / (2.0 * spread * spread)) / gauss_total * inside  6.97 us
    mul x6, other arithmetic, tap_values(): profile * scaled  6.63 us
    dot_general x8, matrix products, place_group(): jnp.einsum('gri,gkip->krp', row_select, broadened_width, precision=larges...  5.76 us
    dot_general x1, matrix products, convolve_all(): fields = jnp.einsum('nkry,nkyz->nrz', smooth, mixed, precision=mxu_value)  4.08 us
    reduce_sum x1, local copies, waits for them, and re-layouts, convolve_all(): jnp.sum(col_ops[None, :, None, :, :, None, :] * fx[:, :, :, :, None, :, :...  3.31 us
  transfers between devices with their start and end apart: 1, of which 1 were waited for; matrix products, arithmetic and copies ran while one was open for 0% of the time, Pallas kernels for 0%

commit v1 on v0

--- a/solution.py
+++ b/solution.py
@@ -11,6 +11,17 @@
 gauss_widths = (0.75, 1.5, 3.0)
 largest_value = lax.Precision.HIGHEST
 mxu_value = lax.Precision.HIGH
+
+
+def cut_along(shard, dim, size):
+    before, after = (shard.shape[:dim], shard.shape[dim + 1 :])
+    return jnp.moveaxis(shard.reshape(*before, size, -1, *after), dim, 0)
+
+
+def laid_out(parts, dim):
+    shape = list(parts.shape[1:])
+    shape[dim] *= parts.shape[0]
+    return jnp.moveaxis(parts, 0, dim).reshape(shape)
 
 
 def tap_values(offsets, kernel_half_width):
@@ -145,7 +156,14 @@
     meta = meta.at[:, 3, :VISITS].set(jnp.broadcast_to(local_count, (devices, VISITS)))
     meta = meta.at[:, 4, :VISITS].set(jnp.broadcast_to(local_load, (devices, VISITS)))
     payload = jnp.concatenate([packed, meta], axis=1)
-    got = lax.all_to_all(payload, "patch", split_axis=0, concat_axis=0, tiled=True)
+    length, here = (lax.axis_size("patch"), lax.axis_index("patch"))
+    blocks = cut_along(payload, 0, length)
+    outs = [blocks[here]]
+    for step in range(1, length):
+        sent = blocks[(here + step) % length]
+        outs.append(lax.ppermute(sent, "patch", [(i, (i + step) % length) for i in range(length)]))
+    blocks = jnp.stack(outs)[(here - jnp.arange(length)) % length]
+    got = laid_out(blocks, 0)
     body_rows = capacity * 2 * strip_rows
     got_meta = got[:, body_rows:, :]
     visit_count = jnp.sum(got_meta[:, 3, :VISITS], axis=0)

time: 93.3 us -> 89 us (0.954)
  the two profiles are of different devices: /device:TPU:0 before, /device:TPU:13 now
where the time goes in v1:
time: 89 us; the launch traced here: 88.4 us
  other arithmetic  24.8 us (28%)
  matrix products  24.6 us (28%)
  waiting for transfers between devices  14.5 us (16%)
  local copies, waits for them, and re-layouts  14.2 us (16%)
  starting transfers between devices  8.67 us (10%)
  between operations  1.31 us (1%)
    ppermute x7, waiting for transfers between devices, shards(): lax.ppermute(sent, 'patch', [(i, (i + step) % length) for i in range(leng...  14.5 us
    dot_general x8, matrix products, place_group(): jnp.einsum('vmwn,vny->vmwy', pixel_block_tile, column_selection, precisio...  11.7 us
    ppermute x7, starting transfers between devices, shards(): lax.ppermute(sent, 'patch', [(i, (i + step) % length) for i in range(leng...  8.67 us
    unnamed x39, local copies, waits for them, and re-layouts  6.92 us
    mul x6, other arithmetic, tap_values(): jnp.exp(-offsets * offsets / (2.0 * spread * spread)) / gauss_total * inside  6.87 us
    mul x6, other arithmetic, tap_values(): profile * scaled  6.55 us
    dot_general x8, matrix products, place_group(): jnp.einsum('gri,gkip->krp', row_select, broadened_width, precision=larges...  5.73 us
    dot_general x1, matrix products, convolve_all(): fields = jnp.einsum('nkry,nkyz->nrz', smooth, mixed, precision=mxu_value)  4.08 us
  transfers between devices with their start and end apart: 7, of which 4 were waited for; matrix products, arithmetic and copies ran while one was open for 5% of the time, Pallas kernels for 0%

profile of v1, /device:TPU:13, one launch (start us, length us, event | category | flops | bytes accessed | tf_op | source)
XLA Modules:
  0.0 88.4 jit_solution(4236304657659100527)
XLA Ops:
  6.7 1.6 %divide_select_fusion.2 = (f32[1,256,276]{1,2,0:T(8,128)}, f32[1,256,276]{1,2,0:T(8,128)}) fusion(f32[]{:T(128)} %exponential_reduce_fusion.2), kind=kLoop, calls=%fused_computation.56 | loop fusion | flops 918528 | bytes 565252 | tf_op jit(solution)/shard_map/mul | solution.py:33
  8.3 1.5 %fusion.29 = f32[1,256,276]{1,2,0:T(8,128)} fusion(f32[]{:T(128)} %exponential_reduce_fusion.2), kind=kLoop, calls=%fused_computation.65 | loop fusion | flops 847872 | bytes 282628 | tf_op jit(solution)/shard_map/mul | solution.py:35
  9.8 1.6 %divide_select_fusion.1 = (f32[1,256,276]{1,2,0:T(8,128)}, f32[1,256,276]{1,2,0:T(8,128)}) fusion(f32[]{:T(128)} %exponential_reduce_fusion.1), kind=kLoop, calls=%fused_computation.55 | loop fusion | flops 918528 | bytes 565252 | tf_op jit(solution)/shard_map/mul | solution.py:33
  11.5 1.5 %fusion.31 = f32[1,256,276]{1,2,0:T(8,128)} fusion(f32[]{:T(128)} %exponential_reduce_fusion.1), kind=kLoop, calls=%fused_computation.67 | loop fusion | flops 847872 | bytes 282628 | tf_op jit(solution)/shard_map/mul | solution.py:35
  13.0 1.6 %divide_select_fusion = (f32[1,256,276]{1,2,0:T(8,128)}, f32[1,256,276]{1,2,0:T(8,128)}) fusion(f32[]{:T(128)} %exponential_reduce_fusion), kind=kLoop, calls=%fused_computation.54 | loop fusion | flops 918528 | bytes 565252 | tf_op jit(solution)/shard_map/mul | solution.py:33
  14.6 1.5 %fusion.27 = f32[1,256,276]{1,2,0:T(8,128)} fusion(f32[]{:T(128)} %exponential_reduce_fusion), kind=kLoop, calls=%fused_computation.63 | loop fusion | flops 847872 | bytes 282628 | tf_op jit(solution)/shard_map/mul | solution.py:35
  18.4 2.7 %multiply_reduce_fusion = f32[2,3,3,128,3,128]{5,3,4,2,1,0:T(8,128)} fusion(f32[2,3,3,3,3,128]{5,4,3,2,1,0:T(4,128)S(1)} %pad_maximum_fusion.3, f32[3,3,128,128]{3,2,1,0:T(8,128)S(1)} %pad_maximum_fusion.1), kind=kLoop, calls=%fused_computation.21 | loop fusion | flops 4423680 | bytes 4211712 | tf_op jit(solution)/shard_map/reduce_sum | solution.py:70
  21.2 3.3 %copy.65 = f32[2,3,3,128,3,128]{3,5,4,2,1,0:T(8,128)S(1)} copy(f32[2,3,3,128,3,128]{5,3,4,2,1,0:T(8,128)} %multiply_reduce_fusion) | data formatting | bytes 7077888 | tf_op jit(solution)/shard_map/reduce_sum | solution.py:70
  29.7 2.2 %fusion.24 = f32[2,128,9,256]{3,1,2,0:T(8,128)S(1)} fusion(f32[9,256,276,1]{1,2,0,3:T(8,128)S(1)} %bitcast.129, f32[2,256,128]{2,1,0:T(8,128)S(1)} %copy-done.9), kind=kOutput, calls=%fused_computation.52 | convolution fusion | flops 976748544 | bytes 5165056 | tf_op jit(solution)/shard_map/krj,njx->nkrx/dot_general | solution.py:57
  31.9 4.1 %fusion.18 = f32[2,256,384]{2,1,0:T(8,128)S(1)} fusion(f32[2,9,128,384]{2,3,1,0:T(8,128)S(1)} %bitcast.128, f32[2,128,9,256]{3,1,2,0:T(8,128)S(1)} %fusion.24), kind=kOutput, calls=%fused_computation.33 | convolution fusion | flops 1358954496 | bytes 6684672 | tf_op jit(solution)/shard_map/nkry,nkyz->nrz/dot_general | solution.py:72
  42.5 1.3 %collective-permute-start.3 = (f32[1,264,128]{2,1,0:T(8,128)S(1)}, f32[1,264,128]{2,1,0:T(8,128)}, u32[]{:S(2)}, u32[]{:S(2)}) collective-permute-start(f32[1,264,128]{2,1,0:T(8,128)S(1)} %get-tuple-element.175), channel_id=1, source_target_pairs={{0,16},{4,20},{8,24},{12,28},{16,0},{20,4},{24,8},{28,12},{1,17},{... | collective-permute-start | bytes 405512 | tf_op jit(solution)/shard_map/ppermute | solution.py:164
  45.0 1.3 %collective-permute-start.5 = (f32[1,264,128]{2,1,0:T(8,128)S(1)}, f32[1,264,128]{2,1,0:T(8,128)S(1)}, u32[]{:S(2)}, u32[]{:S(2)}) collective-permute-start(f32[1,264,128]{2,1,0:T(8,128)S(1)} %fusion.45), channel_id=1, source_target_pairs={{0,24},{4,28},{8,0},{12,4},{16,8},{20,12},{24,16},{28,20},{1,25},{... | collective-permute-start | bytes 405512 | tf_op jit(solution)/shard_map/ppermute | solution.py:164
  47.2 1.5 %collective-permute-start.6 = (f32[1,264,128]{2,1,0:T(8,128)S(1)}, f32[1,264,128]{2,1,0:T(8,128)S(1)}, u32[]{:S(2)}, u32[]{:S(2)}) collective-permute-start(f32[1,264,128]{2,1,0:T(8,128)S(1)} %get-tuple-element.171), channel_id=1, source_target_pairs={{0,28},{4,0},{8,4},{12,8},{16,12},{20,16},{24,20},{28,24},{1,29},{... | collective-permute-start | bytes 405512 | tf_op jit(solution)/shard_map/ppermute | solution.py:164
  49.6 10.3 %collective-permute-done.2 = f32[1,264,128]{2,1,0:T(8,128)} collective-permute-done((f32[1,264,128]{2,1,0:T(8,128)S(1)}, f32[1,264,128]{2,1,0:T(8,128)}, u32[]{:S(2)}, u32[]{:S(2)}) %collective-permute-start.2) | collective-permute-done | bytes 135200 | tf_op jit(solution)/shard_map/ppermute | solution.py:164
  60.8 2.0 %collective-permute-done.3 = f32[1,264,128]{2,1,0:T(8,128)} collective-permute-done((f32[1,264,128]{2,1,0:T(8,128)S(1)}, f32[1,264,128]{2,1,0:T(8,128)}, u32[]{:S(2)}, u32[]{:S(2)}) %collective-permute-start.3) | collective-permute-done | bytes 135200 | tf_op jit(solution)/shard_map/ppermute | solution.py:164
  68.2 19.2 %while.16 = (s32[]{:T(128)}, f32[2,128,512]{1,2,0:T(8,128)S(1)}, f32[8,16,2,8,128]{4,3,2,1,0:T(8,128)S(1)}, s32[8,16,2]{1,0,2:T(8,128)S(1)}, s32[]{:T(128)}, /*index=5*/s32[]{:T(128)}) while((s32[]{:T(128)}, f32[2,128,512]{1,2,0:T(8,128)S(1)}, f32[8,16,2,8,128]{4,3,2,1,0:T(8,128)S(1)}, s32[8,16,2]{1,0,2:T(8,128)S(1)}, ...), condition=%wide.region_13.14_spmd.clone.clone, body=%wide.region_12.13_spmd.clone.clone.sunk | while | flops 403982464 | bytes 2279127 | solution.py:113
  68.3 1.5 %fusion.82 = f32[16,2,8,512]{3,2,1,0:T(8,128)S(1)} fusion(s32[16,128]{1,0:T(8,128)S(1)} %iota_add_fusion.4, f32[8,16,2,8,128]{4,3,2,1,0:T(8,128)S(1)} %get-tuple-element.244, s32[]{:T(128)} %get-tuple-element.236), kind=kOutput, calls=%fused_computation.6.clone.1 | convolution fusion | flops 202375168 | bytes 663556 | tf_op jit(solution)/shard_map/while/body/eval_jaxpr/vmwn,vny->vmwy/dot_general | solution.py:103
  70.7 1.5 %fusion.82 = f32[16,2,8,512]{3,2,1,0:T(8,128)S(1)} fusion(s32[16,128]{1,0:T(8,128)S(1)} %iota_add_fusion.4, f32[8,16,2,8,128]{4,3,2,1,0:T(8,128)S(1)} %get-tuple-element.244, s32[]{:T(128)} %get-tuple-element.236), kind=kOutput, calls=%fused_computation.6.clone.1 | convolution fusion | flops 202375168 | bytes 663556 | tf_op jit(solution)/shard_map/while/body/eval_jaxpr/vmwn,vny->vmwy/dot_general | solution.py:103
  73.1 1.5 %fusion.82 = f32[16,2,8,512]{3,2,1,0:T(8,128)S(1)} fusion(s32[16,128]{1,0:T(8,128)S(1)} %iota_add_fusion.4, f32[8,16,2,8,128]{4,3,2,1,0:T(8,128)S(1)} %get-tuple-element.244, s32[]{:T(128)} %get-tuple-element.236), kind=kOutput, calls=%fused_computation.6.clone.1 | convolution fusion | flops 202375168 | bytes 663556 | tf_op jit(solution)/shard_map/while/body/eval_jaxpr/vmwn,vny->vmwy/dot_general | solution.py:103
  75.5 1.5 %fusion.82 = f32[16,2,8,512]{3,2,1,0:T(8,128)S(1)} fusion(s32[16,128]{1,0:T(8,128)S(1)} %iota_add_fusion.4, f32[8,16,2,8,128]{4,3,2,1,0:T(8,128)S(1)} %get-tuple-element.244, s32[]{:T(128)} %get-tuple-element.236), kind=kOutput, calls=%fused_computation.6.clone.1 | convolution fusion | flops 202375168 | bytes 663556 | tf_op jit(solution)/shard_map/while/body/eval_jaxpr/vmwn,vny->vmwy/dot_general | solution.py:103
  77.9 1.5 %fusion.82 = f32[16,2,8,512]{3,2,1,0:T(8,128)S(1)} fusion(s32[16,128]{1,0:T(8,128)S(1)} %iota_add_fusion.4, f32[8,16,2,8,128]{4,3,2,1,0:T(8,128)S(1)} %get-tuple-element.244, s32[]{:T(128)} %get-tuple-element.236), kind=kOutput, calls=%fused_computation.6.clone.1 | convolution fusion | flops 202375168 | bytes 663556 | tf_op jit(solution)/shard_map/while/body/eval_jaxpr/vmwn,vny->vmwy/dot_general | solution.py:103
  80.3 1.5 %fusion.82 = f32[16,2,8,512]{3,2,1,0:T(8,128)S(1)} fusion(s32[16,128]{1,0:T(8,128)S(1)} %iota_add_fusion.4, f32[8,16,2,8,128]{4,3,2,1,0:T(8,128)S(1)} %get-tuple-element.244, s32[]{:T(128)} %get-tuple-element.236), kind=kOutput, calls=%fused_computation.6.clone.1 | convolution fusion | flops 202375168 | bytes 663556 | tf_op jit(solution)/shard_map/while/body/eval_jaxpr/vmwn,vny->vmwy/dot_general | solution.py:103
  82.7 1.5 %fusion.82 = f32[16,2,8,512]{3,2,1,0:T(8,128)S(1)} fusion(s32[16,128]{1,0:T(8,128)S(1)} %iota_add_fusion.4, f32[8,16,2,8,128]{4,3,2,1,0:T(8,128)S(1)} %get-tuple-element.244, s32[]{:T(128)} %get-tuple-element.236), kind=kOutput, calls=%fused_computation.6.clone.1 | convolution fusion | flops 202375168 | bytes 663556 | tf_op jit(solution)/shard_map/while/body/eval_jaxpr/vmwn,vny->vmwy/dot_general | solution.py:103
  85.1 1.5 %fusion.82 = f32[16,2,8,512]{3,2,1,0:T(8,128)S(1)} fusion(s32[16,128]{1,0:T(8,128)S(1)} %iota_add_fusion.4, f32[8,16,2,8,128]{4,3,2,1,0:T(8,128)S(1)} %get-tuple-element.244, s32[]{:T(128)} %get-tuple-element.236), kind=kOutput, calls=%fused_computation.6.clone.1 | convolution fusion | flops 202375168 | bytes 663556 | tf_op jit(solution)/shard_map/while/body/eval_jaxpr/vmwn,vny->vmwy/dot_general | solution.py:103
  (170 shorter events, 37.0 us)
Async XLA Ops:
  8.3 7.7 %copy-start.10 = (f32[2,27,6]{1,0,2:T(2,128)S(1)}, f32[2,27,6]{1,0,2:T(2,128)}, u32[]{:S(2)}) copy-start(f32[2,27,6]{1,0,2:T(2,128)} %param.19) | copy-start | bytes 3892
  24.5 2.9 %copy-start = (f32[1,256,276]{1,2,0:T(8,128)S(1)}, f32[1,256,276]{1,2,0:T(8,128)}, u32[]{:S(2)}) copy-start(f32[1,256,276]{1,2,0:T(8,128)} %fusion.29) | copy-start | bytes 847876
  24.5 2.9 %copy-start.3 = (f32[1,256,276]{1,2,0:T(8,128)S(1)}, f32[1,256,276]{1,2,0:T(8,128)}, u32[]{:S(2)}) copy-start(f32[1,256,276]{1,2,0:T(8,128)} %get-tuple-element.195) | copy-start | bytes 847876
  24.5 2.9 %copy-start.4 = (f32[1,256,276]{1,2,0:T(8,128)S(1)}, f32[1,256,276]{1,2,0:T(8,128)}, u32[]{:S(2)}) copy-start(f32[1,256,276]{1,2,0:T(8,128)} %get-tuple-element.196) | copy-start | bytes 847876
  25.8 1.8 %copy-start.1 = (f32[1,256,276]{1,2,0:T(8,128)S(1)}, f32[1,256,276]{1,2,0:T(8,128)}, u32[]{:S(2)}) copy-start(f32[1,256,276]{1,2,0:T(8,128)} %fusion.31) | copy-start | bytes 847876
  25.8 1.8 %copy-start.5 = (f32[1,256,276]{1,2,0:T(8,128)S(1)}, f32[1,256,276]{1,2,0:T(8,128)}, u32[]{:S(2)}) copy-start(f32[1,256,276]{1,2,0:T(8,128)} %get-tuple-element.191) | copy-start | bytes 847876
  25.8 1.8 %copy-start.6 = (f32[1,256,276]{1,2,0:T(8,128)S(1)}, f32[1,256,276]{1,2,0:T(8,128)}, u32[]{:S(2)}) copy-start(f32[1,256,276]{1,2,0:T(8,128)} %get-tuple-element.192) | copy-start | bytes 847876
  27.4 8.8 %copy-start.11 = (s32[64]{0:T(128)}, s32[64]{0:T(128)S(1)}, u32[]{:S(2)}) copy-start(s32[64]{0:T(128)S(1)} %multiply_add_fusion.4) | copy-start | bytes 772
  27.5 1.0 %copy-start.2 = (f32[1,256,276]{1,2,0:T(8,128)S(1)}, f32[1,256,276]{1,2,0:T(8,128)}, u32[]{:S(2)}) copy-start(f32[1,256,276]{1,2,0:T(8,128)} %fusion.27) | copy-start | bytes 847876
  27.5 1.0 %copy-start.7 = (f32[1,256,276]{1,2,0:T(8,128)S(1)}, f32[1,256,276]{1,2,0:T(8,128)}, u32[]{:S(2)}) copy-start(f32[1,256,276]{1,2,0:T(8,128)} %get-tuple-element.187) | copy-start | bytes 847876
  27.5 1.1 %copy-start.8 = (f32[1,256,276]{1,2,0:T(8,128)S(1)}, f32[1,256,276]{1,2,0:T(8,128)}, u32[]{:S(2)}) copy-start(f32[1,256,276]{1,2,0:T(8,128)} %get-tuple-element.188) | copy-start | bytes 847876
  28.7 1.0 %copy-start.9 = (f32[2,256,128]{2,1,0:T(8,128)S(1)}, f32[2,256,128]{2,1,0:T(8,128)}, u32[]{:S(2)}) copy-start(f32[2,256,128]{2,1,0:T(8,128)} %param.16) | copy-start | bytes 786436
  36.9 0.7 copy-start.13
  37.0 0.8 copy-start.12
  37.0 0.8 copy-start.14
  37.0 0.8 copy-start.15
  39.0 6.0 %collective-permute-start = (f32[1,264,128]{2,1,0:T(8,128)S(1)}, f32[1,264,128]{2,1,0:T(8,128)}, u32[]{:S(2)}, u32[]{:S(2)}) collective-permute-start(f32[1,264,128]{2,1,0:T(8,128)S(1)} %get-tuple-element.172), channel_id=1, source_target_pairs={{0,4},{4,8},{8,12},{12,16},{16,20},{20,24},{24,28},{28,0},{1,5},{5... | collective-permute-start | bytes 405512 | tf_op jit(solution)/shard_map/ppermute | solution.py:164
  40.3 7.0 %collective-permute-start.1 = (f32[1,264,128]{2,1,0:T(8,128)S(1)}, f32[1,264,128]{2,1,0:T(8,128)}, u32[]{:S(2)}, u32[]{:S(2)}) collective-permute-start(f32[1,264,128]{2,1,0:T(8,128)S(1)} %get-tuple-element.173), channel_id=1, source_target_pairs={{0,8},{4,12},{8,16},{12,20},{16,24},{20,28},{24,0},{28,4},{1,9},{5... | collective-permute-start | bytes 405512 | tf_op jit(solution)/shard_map/ppermute | solution.py:164
  41.6 18.4 %collective-permute-start.2 = (f32[1,264,128]{2,1,0:T(8,128)S(1)}, f32[1,264,128]{2,1,0:T(8,128)}, u32[]{:S(2)}, u32[]{:S(2)}) collective-permute-start(f32[1,264,128]{2,1,0:T(8,128)S(1)} %get-tuple-element.174), channel_id=1, source_target_pairs={{0,12},{4,16},{8,20},{12,24},{16,28},{20,0},{24,4},{28,8},{1,13},{... | collective-permute-start | bytes 405512 | tf_op jit(solution)/shard_map/ppermute | solution.py:164
  42.5 20.3 %collective-permute-start.3 = (f32[1,264,128]{2,1,0:T(8,128)S(1)}, f32[1,264,128]{2,1,0:T(8,128)}, u32[]{:S(2)}, u32[]{:S(2)}) collective-permute-start(f32[1,264,128]{2,1,0:T(8,128)S(1)} %get-tuple-element.175), channel_id=1, source_target_pairs={{0,16},{4,20},{8,24},{12,28},{16,0},{20,4},{24,8},{28,12},{1,17},{... | collective-permute-start | bytes 405512 | tf_op jit(solution)/shard_map/ppermute | solution.py:164
  43.9 19.9 %collective-permute-start.4 = (f32[1,264,128]{2,1,0:T(8,128)S(1)}, f32[1,264,128]{2,1,0:T(8,128)}, u32[]{:S(2)}, u32[]{:S(2)}) collective-permute-start(f32[1,264,128]{2,1,0:T(8,128)S(1)} %get-tuple-element.176), channel_id=1, source_target_pairs={{0,20},{4,24},{8,28},{12,0},{16,4},{20,8},{24,12},{28,16},{1,21},{... | collective-permute-start | bytes 405512 | tf_op jit(solution)/shard_map/ppermute | solution.py:164
  45.0 20.7 %collective-permute-start.5 = (f32[1,264,128]{2,1,0:T(8,128)S(1)}, f32[1,264,128]{2,1,0:T(8,128)S(1)}, u32[]{:S(2)}, u32[]{:S(2)}) collective-permute-start(f32[1,264,128]{2,1,0:T(8,128)S(1)} %fusion.45), channel_id=1, source_target_pairs={{0,24},{4,28},{8,0},{12,4},{16,8},{20,12},{24,16},{28,20},{1,25},{... | collective-permute-start | bytes 405512 | tf_op jit(solution)/shard_map/ppermute | solution.py:164
  47.2 19.7 %collective-permute-start.6 = (f32[1,264,128]{2,1,0:T(8,128)S(1)}, f32[1,264,128]{2,1,0:T(8,128)S(1)}, u32[]{:S(2)}, u32[]{:S(2)}) collective-permute-start(f32[1,264,128]{2,1,0:T(8,128)S(1)} %get-tuple-element.171), channel_id=1, source_target_pairs={{0,28},{4,0},{8,4},{12,8},{16,12},{20,16},{24,20},{28,24},{1,29},{... | collective-permute-start | bytes 405512 | tf_op jit(solution)/shard_map/ppermute | solution.py:164
